TPU v7x, 512 devices: a whole 4x8x8 slice. The times are simulated.
512 devices in a mesh: blk: 64 (over y, z), mpo: 8 (over x, core).
Axes of the slice: x: 4, y: 8, z: 8, core: 2. Of those that a mesh axis runs over, the one named last changes fastest.
Arguments:
- wave: bfloat16 [6144, 128, 128], P('blk'), may hold values from -6 to 6
- left_env: bfloat16 [8, 64, 128, 128], P('mpo', 'blk'), may hold values from -0.5 to 0.5
- right_env: bfloat16 [8, 64, 128, 128], P('mpo', 'blk'), may hold values from -0.1875 to 0.1875
- right_sector: int32 [6144, 1], P('blk'), may hold values from 0 to 63; in each aligned block of 96 rows (0 to 95, 96 to 191, ...) at most 2 rows name the same one
- right_home: int32 [64], replicated, may hold values from 0 to 63, each once
Outputs:
- product: bfloat16 [6144, 128, 128], P('blk', None, 'mpo')
Inputs may be any that keep to these rules, and one draw needn't show every extreme that they name: `right_sector`: among the 96 blocks of one device (aligned blocks of rows) no right sector appears more than 2 times, and some sector appears exactly 2 times; every sector appears somewhere. `right_home`: each sector has its own storage row.
All inputs are finite; a program needn't handle non-finite values.
Results may differ from a plain program's by a relative error of at most 0.008.
Values may be sent and summed in bfloat16 or wider, within the bound.
No kernel may reach another device: no remote copies, remote signals or barrier semaphores. Data moves between devices by JAX's collectives and lax.ppermute only.
A program may use at most 64 MiB of HBM per device.

v0:
```python
import jax
import jax.numpy as jnp
from jax import lax
from jax.sharding import PartitionSpec as P


def local(wave, left_env, right_env, right_sector, right_home):
    blocks = wave.shape[0]
    sectors = left_env.shape[1]
    local_left = jnp.arange(blocks, dtype=jnp.int32) * sectors // blocks
    places = jnp.take(right_home, right_sector[:, 0], axis=0)
    chosen = jnp.take(left_env[0], local_left, axis=0)
    left = jnp.einsum("bik,bkj->bij", chosen, wave, preferred_element_type=jnp.float32).astype(
        jnp.bfloat16
    )
    every_right = lax.all_gather(right_env[0], "blk", axis=0, tiled=True)
    picked = jnp.take(every_right, places, axis=0)
    terms = jnp.einsum("bik,bjk->bij", left, picked, preferred_element_type=jnp.float32)
    summed = lax.psum_scatter(terms, "mpo", scatter_dimension=2, tiled=True)
    return summed.astype(jnp.bfloat16)


def solution(mesh):
    in_specs = (
        P("blk", None, None),
        P("mpo", "blk", None, None),
        P("mpo", "blk", None, None),
        P("blk", None),
        P(),
    )
    out_specs = P("blk", None, "mpo")
    return jax.shard_map(local, mesh=mesh, in_specs=in_specs, out_specs=out_specs, check_vma=False)
```

profile of v0, /device:TPU:6, one launch (start us, length us, event | category | flops | bytes accessed | tf_op | source)
XLA Modules:
  0.0 162.3 jit_solution(18109808292682006214)
XLA Ops:
  6.5 0.0 copy-start
  6.5 0.0 all-gather.3.cloned.1.call-start
  6.5 0.7 all-gather.3.cloned.1.call-update
  7.3 0.0 reduce-scatter.2.cloned.1.call-start
  7.3 0.8 fusion.17
  8.1 1.6 gather_fusion
  9.7 0.7 and_bitcast_fusion
  10.4 88.1 %all-gather.3.cloned.1.call-done = bf16[64,1,128,128]{3,2,1,0:T(8,128)(2,1)} async-done(((bf16[1,1,128,128]{3,2,1,0:T(8,128)(2,1)}), bf16[64,1,128,128]{3,2,1,0:T(8,128)(2,1)}) %all-gather.3.cloned.1.call-update) | async-done | bytes 2097168 | tf_op jit(solution)/shard_map/all_gather | solution.py:16
  98.5 0.0 copy-start.1
  98.5 4.3 %gather_fusion.1 = bf16[96,128,128]{2,1,0:T(8,128)(2,1)} fusion(bf16[64,128,128]{2,1,0:T(8,128)(2,1)} %bitcast.13, s32[1024]{0:T(1024)S(1)} %pad_clamp_fusion), kind=kCustom, calls=%fused_computation.1 | custom fusion | bytes 6291840 | tf_op jit(solution)/shard_map/jit(_take)/gather | solution.py:17
  102.8 0.0 copy-done
  102.8 0.0 copy-done.1
  102.8 7.8 %fusion = f32[96,128,128]{1,2,0:T(8,128)} fusion(bf16[96,128,128]{2,1,0:T(8,128)(2,1)} %gather_fusion.1, pred[96]{0:T(512)(128)(4,1)S(1)} %get-tuple-element.5, bf16[96,128,128]{2,1,0:T(8,128)(2,1)S(1)} %copy-done, pred[96]{0:T(512)(128)(4,1)S(1)} %compare_and_fusion, bf16[128,128]{1,0:T(8,128)(2,1)S(1)} %bitcast.15), kind=kOutput, calls=%fused_computation.2 | convolution fusion | flops 810024960 | bytes 12615872 | tf_op jit(solution)/shard_map/bik,bjk->bij/dot_general | solution.py:18
  110.6 0.0 reduce-scatter.2.cloned.1.call-update
  110.6 42.9 %reduce-scatter.2.cloned.1.call-done = f32[96,128,16]{1,2,0:T(8,128)} async-done(((f32[96,128,128]{1,2,0:T(8,128)}), f32[96,128,16]{1,2,0:T(8,128)}) %reduce-scatter.2.cloned.1.call-update) | async-done | bytes 786448 | tf_op jit(solution)/shard_map/reduce_scatter | solution.py:19
  153.5 1.9 %convert_element_type.7 = bf16[96,128,16]{1,2,0:T(8,128)(2,1)} convert(f32[96,128,16]{1,2,0:T(8,128)} %reduce-scatter.2.cloned.1.call-done) | non-fusion elementwise | flops 196608 | bytes 1179648 | tf_op jit(solution)/shard_map/convert_element_type | solution.py:20
  (3 shorter events, 0.0 us)
Async XLA Ops:
  6.5 96.3 %copy-start = (bf16[96,128,128]{2,1,0:T(8,128)(2,1)S(1)}, bf16[96,128,128]{2,1,0:T(8,128)(2,1)}, u32[]{:S(2)}) copy-start(bf16[96,128,128]{2,1,0:T(8,128)(2,1)} %param.5) | copy-start | bytes 9437188
  6.5 92.0 %all-gather.3.cloned.1.call-start = ((), (), s32[]{:S(2)}) async-start(), calls=%async_computation.2 | async-start | bytes 2129920 | tf_op jit(solution)/shard_map/all_gather | solution.py:16
  7.3 146.3 %reduce-scatter.2.cloned.1.call-start = ((), (), s32[]{:S(2)}) async-start(), calls=%async_computation.1 | async-start | bytes 7077888 | tf_op jit(solution)/shard_map/reduce_scatter | solution.py:19
  98.5 4.4 %copy-start.1 = (bf16[1,1,128,128]{3,2,1,0:T(8,128)(2,1)S(1)}, bf16[1,1,128,128]{3,2,1,0:T(8,128)(2,1)}, u32[]{:S(2)}) copy-start(bf16[1,1,128,128]{3,2,1,0:T(8,128)(2,1)} %param.6) | copy-start | bytes 98308
Sparse Core Ops, SparseCore 0:
  10.3 88.0 all-gather.2
  110.8 42.7 reduce-scatter.1
where the time goes:
time: 165 us; the launch traced here: 162 us
  waiting for transfers between devices  132 us (80%)
  between operations  13.4 us (8%)
  matrix products  7.78 us (5%)
  local copies, waits for them, and re-layouts  5.94 us (4%)
  other arithmetic  3.45 us (2%)
    all_gather x1, waiting for transfers between devices, local(): every_right = lax.all_gather(right_env[0], 'blk', axis=0, tiled=True)  88.1 us
    reduce_scatter x1, waiting for transfers between devices, local(): summed = lax.psum_scatter(terms, 'mpo', scatter_dimension=2, tiled=True)  42.9 us
    dot_general x1, matrix products, local(): jnp.einsum('bik,bjk->bij', left, picked, preferred_element_type=jnp.float32)  7.78 us
    gather x1, local copies, waits for them, and re-layouts, local(): picked = jnp.take(every_right, places, axis=0)  4.35 us
  transfers between devices with their start and end apart: 2, of which 2 were waited for; matrix products, arithmetic and copies ran while one was open for 2% of the time, Pallas kernels for 0%

commit v1 on v0

v1 whole, which is shorter than its diff:
```python
import jax
import jax.numpy as jnp
from jax import lax
from jax.sharding import PartitionSpec as P


def local(wave, left_env, right_env, right_sector, right_home):
    terms = lax.axis_size("mpo")
    size = wave.shape[1]
    width = size // terms
    mine = lax.all_to_all(right_env[0, 0].reshape(terms, width, size), "mpo", 0, 0, tiled=False)
    table = lax.all_gather(mine, "blk", axis=0, tiled=False)
    table = table.reshape(table.shape[0], terms * width, size)
    lefts = lax.all_gather(left_env[0, 0], "mpo", axis=0, tiled=False)
    places = jnp.take(right_home, right_sector[:, 0], axis=0)
    picked = jnp.take(table, places, axis=0)
    inner = jnp.einsum("brk,bjk->brj", picked, wave, preferred_element_type=jnp.float32)
    inner = inner.astype(jnp.bfloat16).reshape(wave.shape[0], terms, width, size)
    out = jnp.einsum("bwcj,wij->bic", inner, lefts, preferred_element_type=jnp.float32)
    return out.astype(jnp.bfloat16)


def solution(mesh):
    in_specs = (
        P("blk", None, None),
        P("mpo", "blk", None, None),
        P("mpo", "blk", None, None),
        P("blk", None),
        P(),
    )
    out_specs = P("blk", None, "mpo")
    return jax.shard_map(local, mesh=mesh, in_specs=in_specs, out_specs=out_specs, check_vma=False)
```

time: 165 us -> 120 us (0.73); the launches traced: 162 us -> 120 us
  waiting for transfers between devices: 132 us -> 67.2 us
  blocking collectives: 0 us -> 26.4 us
  other arithmetic: 3.45 us -> 1.35 us
  matrix products: 7.78 us -> 5.97 us
    reduce_scatter x1 -> x0, waiting for transfers between devices: 42.9 us -> none  [local(): summed = lax.psum_scatter(terms, 'mpo', scatter_dimension=2, tiled=True)]
    all_gather x1, waiting for transfers between devices: 88.1 us -> 67.1 us  [local(): table = lax.all_gather(mine, 'blk', axis=0, tiled=False)]
    all_to_all x0 -> x1, blocking collectives: none -> 13.4 us  [local(): lax.all_to_all(right_env[0, 0].reshape(terms, width, size), 'mpo', 0, 0,...]
    all_gather x0 -> x1, blocking collectives: none -> 13 us  [local(): lefts = lax.all_gather(left_env[0, 0], 'mpo', axis=0, tiled=False)]
    convert_element_type x1 -> x0, other arithmetic: 1.93 us -> none  [local(): return summed.astype(jnp.bfloat16)]
    dot_general x1 -> x2, matrix products: 7.78 us -> 5.97 us  [the longest x1 4.24 us: local(): jnp.einsum('brk,bjk->brj', picked, wave, preferred_element_type=jnp.float32)]
  transfers between devices with their start and end apart: 2 -> 1, of which waited for: 2 -> 1; matrix products, arithmetic and copies ran while one was open for 2% -> 2% of each run, Pallas kernels for 0% -> 0%
where the time goes in v1:
time: 120 us
  waiting for transfers between devices  67.2 us (56%)
  blocking collectives  26.4 us (22%)
  between operations  13.4 us (11%)
  matrix products  5.97 us (5%)
  local copies, waits for them, and re-layouts  5.87 us (5%)
  other arithmetic  1.35 us (1%)
    all_gather x1, waiting for transfers between devices, local(): table = lax.all_gather(mine, 'blk', axis=0, tiled=False)  67.1 us
    all_to_all x1, blocking collectives, local(): lax.all_to_all(right_env[0, 0].reshape(terms, width, size), 'mpo', 0, 0,...  13.4 us
    all_gather x1, blocking collectives, local(): lefts = lax.all_gather(left_env[0, 0], 'mpo', axis=0, tiled=False)  13 us
    gather x1, local copies, waits for them, and re-layouts, local(): picked = jnp.take(table, places, axis=0)  4.28 us
    dot_general x1, matrix products, local(): jnp.einsum('brk,bjk->brj', picked, wave, preferred_element_type=jnp.float32)  4.24 us
  transfers between devices with their start and end apart: 1, of which 1 were waited for; matrix products, arithmetic and copies ran while one was open for 2% of the time, Pallas kernels for 0%

profile of v1, /device:TPU:6, one launch (start us, length us, event | category | flops | bytes accessed | tf_op | source)
XLA Modules:
  0.0 120.2 jit_solution(1579030015706970045)
XLA Ops:
  6.5 0.0 copy-start
  6.5 0.0 all-gather.4.cloned.1.call-start
  6.5 13.4 %all_to_all.5 = bf16[8,16,128]{2,1,0:T(8,128)(2,1)} all-to-all(bf16[8,16,128]{2,1,0:T(8,128)(2,1)} %bitcast.30), channel_id=1, replica_groups=mesh['blk'=64,'mpo'=8] {'mpo'}, dimensions={0} | all-to-all | bytes 65536 | tf_op jit(solution)/shard_map/all_to_all | solution.py:11
  19.9 0.0 all-gather.4.cloned.1.call-update
  20.0 0.7 fusion.11
  20.6 1.6 %gather_fusion = s32[96]{0:T(128)S(1)} fusion(s32[64]{0:T(128)} %param.9, s32[1024]{0:T(1024)S(1)} %pad_clamp_fusion.1), kind=kCustom, calls=%fused_computation | custom fusion | bytes 1152 | tf_op jit(solution)/shard_map/jit(_take)/gather | solution.py:15
  22.2 0.7 and_bitcast_fusion
  22.9 13.0 %all-gather.1 = bf16[8,1,128,128]{3,2,1,0:T(8,128)(2,1)S(1)} all-gather(bf16[1,1,128,128]{3,2,1,0:T(8,128)(2,1)} %param.6), channel_id=3, replica_groups=mesh['blk'=64,'mpo'=8] {'mpo'}, dimensions={0}, use_global_device_ids=true | all-gather | bytes 294912 | tf_op jit(solution)/shard_map/all_gather | solution.py:14
  35.9 67.1 %all-gather.4.cloned.1.call-done = bf16[512,16,128]{2,1,0:T(8,128)(2,1)} async-done(((bf16[8,16,128]{2,1,0:T(8,128)(2,1)}), bf16[512,16,128]{2,1,0:T(8,128)(2,1)}) %all-gather.4.cloned.1.call-update) | async-done | bytes 2097168 | tf_op jit(solution)/shard_map/all_gather | solution.py:12
  103.1 4.3 %gather_fusion.1 = bf16[96,128,128]{2,1,0:T(8,128)(2,1)} fusion(bf16[64,128,128]{2,1,0:T(8,128)(2,1)} %bitcast.29, s32[1024]{0:T(1024)S(1)} %pad_clamp_fusion), kind=kCustom, calls=%fused_computation.1 | custom fusion | bytes 6291840 | tf_op jit(solution)/shard_map/jit(_take)/gather | solution.py:16
  107.4 0.0 copy-done
  107.4 4.2 %fusion.3 = bf16[96,128,128]{2,1,0:T(8,128)(2,1)S(1)} fusion(bf16[96,128,128]{2,1,0:T(8,128)(2,1)S(1)} %copy-done, bf16[96,128,128]{2,1,0:T(8,128)(2,1)} %gather_fusion.1, pred[96]{0:T(512)(128)(4,1)S(1)} %get-tuple-element.5), kind=kOutput, calls=%fused_computation.5 | convolution fusion | flops 405798912 | bytes 9437280 | tf_op jit(solution)/shard_map/brk,bjk->brj/dot_general | solution.py:17
  111.6 1.7 %fusion.8 = bf16[96,128,16]{1,2,0:T(8,128)(2,1)} fusion(bf16[96,8,16,128]{3,2,1,0:T(8,128)(2,1)S(1)} %bitcast.28, bf16[8,1,128,128]{3,2,1,0:T(8,128)(2,1)S(1)} %all-gather.1), kind=kOutput, calls=%fused_computation.9 | convolution fusion | flops 402849792 | bytes 3801088 | tf_op jit(solution)/shard_map/bwcj,wij->bic/dot_general | solution.py:19
  (2 shorter events, 0.0 us)
Async XLA Ops:
  6.5 100.8 %copy-start = (bf16[96,128,128]{2,1,0:T(8,128)(2,1)S(1)}, bf16[96,128,128]{2,1,0:T(8,128)(2,1)}, u32[]{:S(2)}) copy-start(bf16[96,128,128]{2,1,0:T(8,128)(2,1)} %param.5) | copy-start | bytes 9437188
  6.5 96.5 %all-gather.4.cloned.1.call-start = ((), (), s32[]{:S(2)}) async-start(), calls=%async_computation.1 | async-start | bytes 2129920 | tf_op jit(solution)/shard_map/all_gather | solution.py:12
Sparse Core Ops, SparseCore 0:
  20.1 82.9 all-gather.3

commit v2 on v1

v2 whole, which is shorter than its diff:
```python
import math

import jax
import jax.numpy as jnp
from jax import lax
from jax.sharding import Mesh
from jax.sharding import PartitionSpec as P


def local(wave, left_env, right_env, right_sector, right_home):
    terms = lax.axis_size("mpo")
    inner_size = lax.axis_size("z")
    size = wave.shape[1]
    width = size // terms
    mine = lax.all_to_all(right_env[0, 0].reshape(terms, width, size), "mpo", 0, 0, tiled=False)
    spread = jnp.broadcast_to(mine[None], (inner_size,) + mine.shape)
    row = lax.all_to_all(spread, "z", 0, 0, tiled=False)
    table = lax.all_gather(row, "y", axis=0, tiled=False)
    table = table.reshape(-1, terms * width, size)
    lefts = lax.all_gather(left_env[0, 0], "mpo", axis=0, tiled=False)
    places = jnp.take(right_home, right_sector[:, 0], axis=0)
    picked = jnp.take(table, places, axis=0)
    inner = jnp.einsum("brk,bjk->brj", picked, wave, preferred_element_type=jnp.float32)
    inner = inner.astype(jnp.bfloat16).reshape(wave.shape[0], terms, width, size)
    out = jnp.einsum("bwcj,wij->bic", inner, lefts, preferred_element_type=jnp.float32)
    return out.astype(jnp.bfloat16)


def solution(mesh):
    blocks, terms = mesh.devices.shape
    inner_size = math.isqrt(blocks)
    grid = Mesh(mesh.devices.reshape(blocks // inner_size, inner_size, terms), ("y", "z", "mpo"))
    blk = ("y", "z")
    in_specs = (
        P(blk, None, None),
        P("mpo", blk, None, None),
        P("mpo", blk, None, None),
        P(blk, None),
        P(),
    )
    out_specs = P(blk, None, "mpo")
    return jax.shard_map(local, mesh=grid, in_specs=in_specs, out_specs=out_specs, check_vma=False)
```

time: 120 us -> 93.9 us (0.78)
  waiting for transfers between devices: 67.2 us -> 23.5 us
  blocking collectives: 26.4 us -> 43.5 us
    all_gather x1, waiting for transfers between devices: 67.1 us -> 23.5 us  [local(): table = lax.all_gather(row, 'y', axis=0, tiled=False)]
    all_to_all x0 -> x1, blocking collectives: none -> 17.8 us  [local(): row = lax.all_to_all(spread, 'z', 0, 0, tiled=False)]
  transfers between devices with their start and end apart: 1 -> 1, of which waited for: 1 -> 1; matrix products, arithmetic and copies ran while one was open for 2% -> 3% of each run, Pallas kernels for 0% -> 0%
where the time goes in v2:
time: 93.9 us; the launch traced here: 93.6 us
  blocking collectives  43.5 us (46%)
  waiting for transfers between devices  23.5 us (25%)
  between operations  13.4 us (14%)
  matrix products  5.96 us (6%)
  local copies, waits for them, and re-layouts  5.9 us (6%)
  other arithmetic  1.35 us (1%)
    all_gather x1, waiting for transfers between devices, local(): table = lax.all_gather(row, 'y', axis=0, tiled=False)  23.5 us
    all_to_all x1, blocking collectives, local(): row = lax.all_to_all(spread, 'z', 0, 0, tiled=False)  17.8 us
    all_gather x1, blocking collectives, local(): lefts = lax.all_gather(left_env[0, 0], 'mpo', axis=0, tiled=False)  13 us
    all_to_all x1, blocking collectives, local(): lax.all_to_all(right_env[0, 0].reshape(terms, width, size), 'mpo', 0, 0,...  12.7 us
    gather x1, local copies, waits for them, and re-layouts, local(): picked = jnp.take(table, places, axis=0)  4.28 us
    dot_general x1, matrix products, local(): jnp.einsum('brk,bjk->brj', picked, wave, preferred_element_type=jnp.float32)  4.23 us
  transfers between devices with their start and end apart: 1, of which 1 were waited for; matrix products, arithmetic and copies ran while one was open for 3% of the time, Pallas kernels for 0%

profile of v2, /device:TPU:6, one launch (start us, length us, event | category | flops | bytes accessed | tf_op | source)
XLA Modules:
  0.0 93.6 jit_solution(7486905566855706745)
XLA Ops:
  6.5 0.0 copy-start
  6.5 0.0 all-gather.4.cloned.1.call-start
  6.5 12.7 %all_to_all.10 = bf16[8,16,128]{2,1,0:T(8,128)(2,1)S(1)} all-to-all(bf16[8,16,128]{2,1,0:T(8,128)(2,1)} %bitcast.30), channel_id=1, replica_groups=mesh['y'=8,'z'=8,'mpo'=8] {'mpo'}, dimensions={0} | all-to-all | bytes 65536 | tf_op jit(solution)/shard_map/all_to_all | solution.py:15
  19.3 17.8 %all_to_all.11 = bf16[8,8,16,128]{3,2,1,0:T(8,128)(2,1)} all-to-all(bf16[8,8,16,128]{3,2,1,0:T(8,128)(2,1)S(1)} %broadcast_in_dim.24), channel_id=1, replica_groups=mesh['y'=8,'z'=8,'mpo'=8] {'z'}, dimensions={0} | all-to-all | bytes 524288 | tf_op jit(solution)/shard_map/all_to_all | solution.py:17
  37.0 0.0 all-gather.4.cloned.1.call-update
  37.1 0.7 fusion.11
  37.7 1.6 %gather_fusion = s32[96]{0:T(128)S(1)} fusion(s32[64]{0:T(128)} %param.9, s32[1024]{0:T(1024)S(1)} %pad_clamp_fusion.1), kind=kCustom, calls=%fused_computation | custom fusion | bytes 1152 | tf_op jit(solution)/shard_map/jit(_take)/gather | solution.py:21
  39.3 0.7 and_bitcast_fusion
  40.0 13.0 %all-gather.1 = bf16[8,1,128,128]{3,2,1,0:T(8,128)(2,1)S(1)} all-gather(bf16[1,1,128,128]{3,2,1,0:T(8,128)(2,1)} %param.6), channel_id=3, replica_groups=mesh['y'=8,'z'=8,'mpo'=8] {'mpo'}, dimensions={0}, use_global_device_ids=true | all-gather | bytes 294912 | tf_op jit(solution)/shard_map/all_gather | solution.py:20
  53.0 23.5 %all-gather.4.cloned.1.call-done = bf16[64,8,16,128]{3,2,1,0:T(8,128)(2,1)} async-done(((bf16[8,8,16,128]{3,2,1,0:T(8,128)(2,1)}), bf16[64,8,16,128]{3,2,1,0:T(8,128)(2,1)}) %all-gather.4.cloned.1.call-update) | async-done | bytes 2097168 | tf_op jit(solution)/shard_map/all_gather | solution.py:18
  76.5 4.3 %gather_fusion.1 = bf16[96,128,128]{2,1,0:T(8,128)(2,1)} fusion(bf16[64,128,128]{2,1,0:T(8,128)(2,1)} %bitcast.29, s32[1024]{0:T(1024)S(1)} %pad_clamp_fusion), kind=kCustom, calls=%fused_computation.1 | custom fusion | bytes 6291840 | tf_op jit(solution)/shard_map/jit(_take)/gather | solution.py:22
  80.8 0.0 copy-done
  80.8 4.2 %fusion.3 = bf16[96,128,128]{2,1,0:T(8,128)(2,1)S(1)} fusion(bf16[96,128,128]{2,1,0:T(8,128)(2,1)S(1)} %copy-done, bf16[96,128,128]{2,1,0:T(8,128)(2,1)} %gather_fusion.1, pred[96]{0:T(512)(128)(4,1)S(1)} %get-tuple-element.5), kind=kOutput, calls=%fused_computation.5 | convolution fusion | flops 405798912 | bytes 9437280 | tf_op jit(solution)/shard_map/brk,bjk->brj/dot_general | solution.py:23
  85.0 1.7 %fusion.8 = bf16[96,128,16]{1,2,0:T(8,128)(2,1)} fusion(bf16[96,8,16,128]{3,2,1,0:T(8,128)(2,1)S(1)} %bitcast.28, bf16[8,1,128,128]{3,2,1,0:T(8,128)(2,1)S(1)} %all-gather.1), kind=kOutput, calls=%fused_computation.9 | convolution fusion | flops 402849792 | bytes 3801088 | tf_op jit(solution)/shard_map/bwcj,wij->bic/dot_general | solution.py:25
  (3 shorter events, 0.0 us)
Async XLA Ops:
  6.5 74.3 %copy-start = (bf16[96,128,128]{2,1,0:T(8,128)(2,1)S(1)}, bf16[96,128,128]{2,1,0:T(8,128)(2,1)}, u32[]{:S(2)}) copy-start(bf16[96,128,128]{2,1,0:T(8,128)(2,1)} %param.5) | copy-start | bytes 9437188
  6.5 70.0 %all-gather.4.cloned.1.call-start = ((), (), s32[]{:S(2)}) async-start(), calls=%async_computation.2 | async-start | bytes 2359296 | tf_op jit(solution)/shard_map/all_gather | solution.py:18
Sparse Core Ops, SparseCore 0:
  37.2 39.3 all-gather.3

commit v3 on v2

--- a/solution.py
+++ b/solution.py
@@ -12,9 +12,9 @@
     inner_size = lax.axis_size("z")
     size = wave.shape[1]
     width = size // terms
-    mine = lax.all_to_all(right_env[0, 0].reshape(terms, width, size), "mpo", 0, 0, tiled=False)
-    spread = jnp.broadcast_to(mine[None], (inner_size,) + mine.shape)
-    row = lax.all_to_all(spread, "z", 0, 0, tiled=False)
+    own = right_env[0, 0].reshape(1, terms, width, size)
+    spread = jnp.broadcast_to(own, (inner_size, terms, width, size)).reshape(inner_size * terms, width, size)
+    row = lax.all_to_all(spread, ("z", "mpo"), 0, 0, tiled=True)
     table = lax.all_gather(row, "y", axis=0, tiled=False)
     table = table.reshape(-1, terms * width, size)
     lefts = lax.all_gather(left_env[0, 0], "mpo", axis=0, tiled=False)

time: 93.9 us -> 90.7 us (0.966)
  blocking collectives: 43.5 us -> 38.7 us
    all_to_all x2 -> x1, blocking collectives: 30.5 us -> 25.6 us  [local(): row = lax.all_to_all(spread, ('z', 'mpo'), 0, 0, tiled=True)]
where the time goes in v3:
time: 90.7 us; the launch traced here: 90.5 us
  blocking collectives  38.7 us (43%)
  waiting for transfers between devices  24.2 us (27%)
  between operations  13.4 us (15%)
  local copies, waits for them, and re-layouts  6.81 us (8%)
  matrix products  5.97 us (7%)
  other arithmetic  1.35 us (1%)
    all_to_all x1, blocking collectives, local(): row = lax.all_to_all(spread, ('z', 'mpo'), 0, 0, tiled=True)  25.6 us
    all_gather x1, waiting for transfers between devices, local(): table = lax.all_gather(row, 'y', axis=0, tiled=False)  24.2 us
    all_gather x1, blocking collectives, local(): lefts = lax.all_gather(left_env[0, 0], 'mpo', axis=0, tiled=False)  13 us
    gather x1, local copies, waits for them, and re-layouts, local(): picked = jnp.take(table, places, axis=0)  4.28 us
    dot_general x1, matrix products, local(): jnp.einsum('brk,bjk->brj', picked, wave, preferred_element_type=jnp.float32)  4.24 us
  transfers between devices with their start and end apart: 1, of which 1 were waited for; matrix products, arithmetic and copies ran while one was open for 3% of the time, Pallas kernels for 0%

profile of v3, /device:TPU:6, one launch (start us, length us, event | category | flops | bytes accessed | tf_op | source)
XLA Modules:
  0.0 90.5 jit_solution(13838994189927755469)
XLA Ops:
  6.5 0.0 copy-start
  6.5 0.0 all-gather.4.cloned.1.call-start
  6.5 0.9 %broadcast_in_dim.26 = bf16[8,8,16,128]{3,2,1,0:T(8,128)(2,1)S(1)} broadcast(bf16[8,16,128]{2,1,0:T(8,128)(2,1)} %bitcast.32), dimensions={1,2,3} | broadcast | bytes 294912 | tf_op jit(solution)/shard_map/broadcast_in_dim | solution.py:16
  7.5 25.6 %all_to_all.5 = bf16[64,16,128]{2,1,0:T(8,128)(2,1)} all-to-all(bf16[64,16,128]{2,1,0:T(8,128)(2,1)S(1)} %bitcast.31), channel_id=1, replica_groups=mesh['y'=8,'z'=8,'mpo'=8] {'z','mpo'}, dimensions={0} | all-to-all | bytes 524288 | tf_op jit(solution)/shard_map/all_to_all | solution.py:17
  33.1 0.0 all-gather.4.cloned.1.call-update
  33.2 0.7 fusion.11
  33.8 1.6 %gather_fusion = s32[96]{0:T(128)S(1)} fusion(s32[64]{0:T(128)} %param.9, s32[1024]{0:T(1024)S(1)} %pad_clamp_fusion.1), kind=kCustom, calls=%fused_computation | custom fusion | bytes 1152 | tf_op jit(solution)/shard_map/jit(_take)/gather | solution.py:21
  35.4 0.7 and_bitcast_fusion
  36.1 13.0 %all-gather.1 = bf16[8,1,128,128]{3,2,1,0:T(8,128)(2,1)S(1)} all-gather(bf16[1,1,128,128]{3,2,1,0:T(8,128)(2,1)} %param.6), channel_id=3, replica_groups=mesh['y'=8,'z'=8,'mpo'=8] {'mpo'}, dimensions={0}, use_global_device_ids=true | all-gather | bytes 294912 | tf_op jit(solution)/shard_map/all_gather | solution.py:20
  49.1 24.2 %all-gather.4.cloned.1.call-done = bf16[512,16,128]{2,1,0:T(8,128)(2,1)} async-done(((bf16[64,16,128]{2,1,0:T(8,128)(2,1)}), bf16[512,16,128]{2,1,0:T(8,128)(2,1)}) %all-gather.4.cloned.1.call-update) | async-done | bytes 2097168 | tf_op jit(solution)/shard_map/all_gather | solution.py:18
  73.4 4.3 %gather_fusion.1 = bf16[96,128,128]{2,1,0:T(8,128)(2,1)} fusion(bf16[64,128,128]{2,1,0:T(8,128)(2,1)} %bitcast.30, s32[1024]{0:T(1024)S(1)} %pad_clamp_fusion), kind=kCustom, calls=%fused_computation.1 | custom fusion | bytes 6291840 | tf_op jit(solution)/shard_map/jit(_take)/gather | solution.py:22
  77.6 0.0 copy-done
  77.6 4.2 %fusion.3 = bf16[96,128,128]{2,1,0:T(8,128)(2,1)S(1)} fusion(bf16[96,128,128]{2,1,0:T(8,128)(2,1)S(1)} %copy-done, bf16[96,128,128]{2,1,0:T(8,128)(2,1)} %gather_fusion.1, pred[96]{0:T(512)(128)(4,1)S(1)} %get-tuple-element.5), kind=kOutput, calls=%fused_computation.5 | convolution fusion | flops 405798912 | bytes 9437280 | tf_op jit(solution)/shard_map/brk,bjk->brj/dot_general | solution.py:23
  81.9 1.7 %fusion.8 = bf16[96,128,16]{1,2,0:T(8,128)(2,1)} fusion(bf16[96,8,16,128]{3,2,1,0:T(8,128)(2,1)S(1)} %bitcast.29, bf16[8,1,128,128]{3,2,1,0:T(8,128)(2,1)S(1)} %all-gather.1), kind=kOutput, calls=%fused_computation.9 | convolution fusion | flops 402849792 | bytes 3801088 | tf_op jit(solution)/shard_map/bwcj,wij->bic/dot_general | solution.py:25
  (2 shorter events, 0.0 us)
Async XLA Ops:
  6.5 71.1 %copy-start = (bf16[96,128,128]{2,1,0:T(8,128)(2,1)S(1)}, bf16[96,128,128]{2,1,0:T(8,128)(2,1)}, u32[]{:S(2)}) copy-start(bf16[96,128,128]{2,1,0:T(8,128)(2,1)} %param.5) | copy-start | bytes 9437188
  6.5 66.8 %all-gather.4.cloned.1.call-start = ((), (), s32[]{:S(2)}) async-start(), calls=%async_computation.1 | async-start | bytes 2359296 | tf_op jit(solution)/shard_map/all_gather | solution.py:18
Sparse Core Ops, SparseCore 0:
  33.3 40.0 all-gather.3

commit v4 on v3

--- a/solution.py
+++ b/solution.py
@@ -1,10 +1,56 @@
 import math
+
+import functools
 
 import jax
 import jax.numpy as jnp
 from jax import lax
+from jax.experimental import pallas as pl
+from jax.experimental.pallas import tpu as pltpu
 from jax.sharding import Mesh
 from jax.sharding import PartitionSpec as P
+
+
+def tail_kernel(group, terms, width, places_ref, table_ref, wave_ref, lefts_ref, out_ref, inner_ref):
+    step = pl.program_id(0)
+    contract = (((1,), (1,)), ((), ()))
+    for g in range(group):
+        rows = table_ref[places_ref[step * group + g]]
+        inner = lax.dot_general(rows, wave_ref[g], contract, preferred_element_type=jnp.float32)
+        inner_ref[g] = inner.astype(inner_ref.dtype)
+    total = None
+    for w in range(terms):
+        part = inner_ref[:, w * width : (w + 1) * width, :].reshape(group * width, -1)
+        term = lax.dot_general(part, lefts_ref[w], contract, preferred_element_type=jnp.float32)
+        total = term if total is None else total + term
+    out_ref[...] = total.reshape(out_ref.shape).astype(out_ref.dtype)
+
+
+def tail(places, table, wave, lefts, terms, width):
+    blocks, size, _ = wave.shape
+    group = 8
+    kernel = functools.partial(tail_kernel, group, terms, width)
+    spec = pltpu.PrefetchScalarGridSpec(
+        num_scalar_prefetch=1,
+        grid=(blocks // group,),
+        in_specs=[
+            pl.BlockSpec(table.shape, lambda i, p: (0, 0, 0)),
+            pl.BlockSpec((group, size, size), lambda i, p: (i, 0, 0)),
+            pl.BlockSpec(lefts.shape, lambda i, p: (0, 0, 0)),
+        ],
+        out_specs=pl.BlockSpec((group, width, size), lambda i, p: (i, 0, 0)),
+        scratch_shapes=[pltpu.VMEM((group, size, size), jnp.bfloat16)],
+    )
+    flops = 4 * blocks * size * size * size
+    moved = 2 * (table.size + wave.size + lefts.size + blocks * width * size)
+    out = pl.pallas_call(
+        kernel,
+        grid_spec=spec,
+        out_shape=jax.ShapeDtypeStruct((blocks, width, size), jnp.bfloat16),
+        compiler_params=pltpu.CompilerParams(dimension_semantics=("arbitrary",)),
+        cost_estimate=pl.CostEstimate(flops=flops, bytes_accessed=moved, transcendentals=0),
+    )(places, table, wave, lefts)
+    return jnp.swapaxes(out, 1, 2)
 
 
 def local(wave, left_env, right_env, right_sector, right_home):
@@ -19,11 +65,7 @@
     table = table.reshape(-1, terms * width, size)
     lefts = lax.all_gather(left_env[0, 0], "mpo", axis=0, tiled=False)
     places = jnp.take(right_home, right_sector[:, 0], axis=0)
-    picked = jnp.take(table, places, axis=0)
-    inner = jnp.einsum("brk,bjk->brj", picked, wave, preferred_element_type=jnp.float32)
-    inner = inner.astype(jnp.bfloat16).reshape(wave.shape[0], terms, width, size)
-    out = jnp.einsum("bwcj,wij->bic", inner, lefts, preferred_element_type=jnp.float32)
-    return out.astype(jnp.bfloat16)
+    return tail(places.astype(jnp.int32), table, wave, lefts, terms, width)
 
 
 def solution(mesh):

time: 90.7 us -> 93.8 us (1.034)
  Pallas kernels: 0 us -> 13.2 us
  matrix products: 5.97 us -> 0 us
  local copies, waits for them, and re-layouts: 6.81 us -> 2.03 us
  waiting for transfers between devices: 24.2 us -> 22.9 us
  blocking collectives: 38.7 us -> 39.8 us
    pallas_call x0 -> x1, Pallas kernels: none -> 13.2 us  [tail(): pl.pallas_call(kernel, grid_spec=spec, out_shape=jax.ShapeDtypeStruct((bl...]
    dot_general x2 -> x0, matrix products: 5.97 us -> none  [the longest x1 4.24 us: local(): jnp.einsum('brk,bjk->brj', picked, wave, preferred_element_type=jnp.float32)]
    gather x1 -> x0, local copies, waits for them, and re-layouts: 4.28 us -> none  [local(): picked = jnp.take(table, places, axis=0)]
    all_gather x1, waiting for transfers between devices: 24.2 us -> 22.9 us  [local(): table = lax.all_gather(row, 'y', axis=0, tiled=False)]
    select_n x1 -> x2, other arithmetic: 0.66 us -> 1.91 us  [local(): places = jnp.take(right_home, right_sector[:, 0], axis=0)]
    all_gather x1, blocking collectives: 13 us -> 14.1 us  [local(): lefts = lax.all_gather(left_env[0, 0], 'mpo', axis=0, tiled=False)]
where the time goes in v4:
time: 93.8 us; the launch traced here: 93.3 us
  blocking collectives  39.8 us (42%)
  waiting for transfers between devices  22.9 us (24%)
  between operations  13.4 us (14%)
  Pallas kernels  13.2 us (14%)
  local copies, waits for them, and re-layouts  2.03 us (2%)
  other arithmetic  1.92 us (2%)
    all_to_all x1, blocking collectives, local(): row = lax.all_to_all(spread, ('z', 'mpo'), 0, 0, tiled=True)  25.6 us
    all_gather x1, waiting for transfers between devices, local(): table = lax.all_gather(row, 'y', axis=0, tiled=False)  22.9 us
    all_gather x1, blocking collectives, local(): lefts = lax.all_gather(left_env[0, 0], 'mpo', axis=0, tiled=False)  14.1 us
    pallas_call x1, Pallas kernels, tail(): pl.pallas_call(kernel, grid_spec=spec, out_shape=jax.ShapeDtypeStruct((bl...  13.2 us
    select_n x2, other arithmetic, local(): places = jnp.take(right_home, right_sector[:, 0], axis=0)  1.91 us
  transfers between devices with their start and end apart: 1, of which 1 were waited for; matrix products, arithmetic and copies ran while one was open for 3% of the time, Pallas kernels for 0%

profile of v4, /device:TPU:6, one launch (start us, length us, event | category | flops | bytes accessed | tf_op | source)
XLA Modules:
  0.0 93.3 jit_solution(9664283957363542734)
XLA Ops:
  6.5 0.0 copy-start
  6.5 0.0 all-gather.4.cloned.1.call-start
  6.5 0.8 broadcast_in_dim.15
  7.3 25.6 %all_to_all.5 = bf16[64,16,128]{2,1,0:T(8,128)(2,1)} all-to-all(bf16[64,16,128]{2,1,0:T(8,128)(2,1)S(1)} %bitcast.11), channel_id=1, replica_groups=mesh['y'=8,'z'=8,'mpo'=8] {'z','mpo'}, dimensions={0} | all-to-all | bytes 524288 | tf_op jit(solution)/shard_map/all_to_all | solution.py:63
  33.0 0.0 all-gather.4.cloned.1.call-update
  33.0 0.7 fusion
  33.7 0.0 copy-done
  33.7 1.2 %gather_fusion = s32[96]{0:T(128)S(1)} fusion(s32[64]{0:T(128)S(1)} %copy-done, s32[1024]{0:T(1024)S(1)} %pad_clamp_fusion), kind=kCustom, calls=%fused_computation | custom fusion | bytes 1152 | tf_op jit(solution)/shard_map/jit(_take)/gather | solution.py:67
  34.9 14.1 %all-gather.1 = bf16[8,1,128,128]{3,2,1,0:T(8,128)(2,1)} all-gather(bf16[1,1,128,128]{3,2,1,0:T(8,128)(2,1)} %param.6), channel_id=3, replica_groups=mesh['y'=8,'z'=8,'mpo'=8] {'mpo'}, dimensions={0}, use_global_device_ids=true | all-gather | bytes 294912 | tf_op jit(solution)/shard_map/all_gather | solution.py:66
  49.0 1.2 %bitcast_select_fusion.places_ref = s32[96]{0:T(128)} fusion(s32[96]{0:T(128)S(1)} %gather_fusion, s32[96,1]{0,1:T(1,128)} %param.8), kind=kLoop, calls=%fused_computation.3 | loop fusion | flops 672 | bytes 1152 | tf_op jit(solution)/shard_map/jit(_take)/select_n | solution.py:67
  50.3 22.9 %all-gather.4.cloned.1.call-done = bf16[512,16,128]{2,1,0:T(8,128)(2,1)} async-done(((bf16[64,16,128]{2,1,0:T(8,128)(2,1)}), bf16[512,16,128]{2,1,0:T(8,128)(2,1)}) %all-gather.4.cloned.1.call-update) | async-done | bytes 2097168 | tf_op jit(solution)/shard_map/all_gather | solution.py:64
  73.2 13.2 %shard_map.55 = bf16[96,16,128]{2,1,0:T(8,128)(2,1)} custom-call(s32[96]{0:T(128)} %bitcast_select_fusion.places_ref, bf16[64,128,128]{2,1,0:T(8,128)(2,1)} %bitcast.9, bf16[96,128,128]{2,1,0:T(8,128)(2,1)} %wave_ref.1, bf16[8,128,128]{2,1,0:T(8,128)(2,1)} %bitcast.10), custom_call_target="tpu_custom_call" | custom-call | flops 805306368 | bytes 5898240 | tf_op jit(solution)/shard_map/pallas_call | solution.py:46
  (1 shorter events, 0.0 us)
Async XLA Ops:
  6.5 27.2 %copy-start = (s32[64]{0:T(128)S(1)}, s32[64]{0:T(128)}, u32[]{:S(2)}) copy-start(s32[64]{0:T(128)} %param.9) | copy-start | bytes 772
  6.5 66.7 %all-gather.4.cloned.1.call-start = ((), (), s32[]{:S(2)}) async-start(), calls=%async_computation.1 | async-start | bytes 2359296 | tf_op jit(solution)/shard_map/all_gather | solution.py:64
Sparse Core Ops, SparseCore 0:
  33.1 40.0 all-gather.3

commit v5 on v3

--- a/solution.py
+++ b/solution.py
@@ -19,11 +19,19 @@
     table = table.reshape(-1, terms * width, size)
     lefts = lax.all_gather(left_env[0, 0], "mpo", axis=0, tiled=False)
     places = jnp.take(right_home, right_sector[:, 0], axis=0)
-    picked = jnp.take(table, places, axis=0)
-    inner = jnp.einsum("brk,bjk->brj", picked, wave, preferred_element_type=jnp.float32)
-    inner = inner.astype(jnp.bfloat16).reshape(wave.shape[0], terms, width, size)
-    out = jnp.einsum("bwcj,wij->bic", inner, lefts, preferred_element_type=jnp.float32)
-    return out.astype(jnp.bfloat16)
+    blocks = wave.shape[0]
+    rows = table.shape[0]
+    cap = 2
+    order = jnp.arange(blocks)
+    rank = jnp.sum((places[:, None] == places[None, :]) & (order[:, None] > order[None, :]), axis=1)
+    slot = places * cap + rank
+    owner = jnp.full((rows * cap,), blocks, jnp.int32).at[slot].set(order.astype(jnp.int32))
+    slotted = jnp.take(wave, owner, axis=0, mode="clip").reshape(rows, cap, size, size)
+    inner = jnp.einsum("prk,psjk->psrj", table, slotted, preferred_element_type=jnp.float32)
+    inner = inner.astype(jnp.bfloat16).reshape(rows, cap, terms, width, size)
+    out = jnp.einsum("pswcj,wij->psci", inner, lefts, preferred_element_type=jnp.float32)
+    out = jnp.take(out.astype(jnp.bfloat16).reshape(rows * cap, width, size), slot, axis=0, mode="clip")
+    return jnp.swapaxes(out, 1, 2)
 
 
 def solution(mesh):

time: 90.7 us -> 89.1 us (0.982)
  waiting for transfers between devices: 24.2 us -> 20.4 us
  local copies, waits for them, and re-layouts: 6.81 us -> 8.87 us
    all_gather x1, waiting for transfers between devices: 24.2 us -> 20.4 us  [local(): table = lax.all_gather(row, 'y', axis=0, tiled=False)]
    gather x1 -> x2, local copies, waits for them, and re-layouts: 4.28 us -> 5.46 us  [the longest x1 3.02 us: local(): jnp.take(wave, owner, axis=0, mode='clip').reshape(rows, cap, size, size)]
  transfers between devices with their start and end apart: 1 -> 1, of which waited for: 1 -> 1; matrix products, arithmetic and copies ran while one was open for 3% -> 8% of each run, Pallas kernels for 0% -> 0%
where the time goes in v5:
time: 89.1 us; the launch traced here: 88.9 us
  blocking collectives  38.5 us (43%)
  waiting for transfers between devices  20.4 us (23%)
  between operations  13.5 us (15%)
  local copies, waits for them, and re-layouts  8.87 us (10%)
  matrix products  6.17 us (7%)
  other arithmetic  1.54 us (2%)
    all_to_all x1, blocking collectives, local(): row = lax.all_to_all(spread, ('z', 'mpo'), 0, 0, tiled=True)  25.6 us
    all_gather x1, waiting for transfers between devices, local(): table = lax.all_gather(row, 'y', axis=0, tiled=False)  20.4 us
    all_gather x1, blocking collectives, local(): lefts = lax.all_gather(left_env[0, 0], 'mpo', axis=0, tiled=False)  12.8 us
    dot_general x1, matrix products, local(): jnp.einsum('prk,psjk->psrj', table, slotted, preferred_element_type=jnp.f...  4.12 us
    gather x1, local copies, waits for them, and re-layouts, local(): jnp.take(wave, owner, axis=0, mode='clip').reshape(rows, cap, size, size)  3.02 us
    gather x1, local copies, waits for them, and re-layouts, local(): jnp.take(out.astype(jnp.bfloat16).reshape(rows * cap, width, size), slot,...  2.44 us
    dot_general x1, matrix products, local(): jnp.einsum('pswcj,wij->psci', inner, lefts, preferred_element_type=jnp.fl...  2.05 us
  transfers between devices with their start and end apart: 1, of which 1 were waited for; matrix products, arithmetic and copies ran while one was open for 8% of the time, Pallas kernels for 0%

profile of v5, /device:TPU:6, one launch (start us, length us, event | category | flops | bytes accessed | tf_op | source)
XLA Modules:
  0.0 88.9 jit_solution(726451716935248667)
XLA Ops:
  6.5 0.0 copy-start
  6.5 0.0 all-gather.4.cloned.1.call-start
  6.5 0.9 %broadcast_in_dim.34 = bf16[8,8,16,128]{3,2,1,0:T(8,128)(2,1)S(1)} broadcast(bf16[8,16,128]{2,1,0:T(8,128)(2,1)} %bitcast.52), dimensions={1,2,3} | broadcast | bytes 294912 | tf_op jit(solution)/shard_map/broadcast_in_dim | solution.py:16
  7.5 25.6 %all_to_all.5 = bf16[64,16,128]{2,1,0:T(8,128)(2,1)} all-to-all(bf16[64,16,128]{2,1,0:T(8,128)(2,1)S(1)} %bitcast.51), channel_id=1, replica_groups=mesh['y'=8,'z'=8,'mpo'=8] {'z','mpo'}, dimensions={0} | all-to-all | bytes 524288 | tf_op jit(solution)/shard_map/all_to_all | solution.py:17
  33.1 0.0 all-gather.4.cloned.1.call-update
  33.2 0.7 fusion.7
  33.8 1.6 %gather_fusion = s32[96]{0:T(128)S(1)} fusion(s32[64]{0:T(128)} %param.9, s32[1024]{0:T(1024)S(1)} %pad_clamp_fusion.2), kind=kCustom, calls=%fused_computation | custom fusion | bytes 1152 | tf_op jit(solution)/shard_map/jit(_take)/gather | solution.py:21
  35.4 0.7 fusion.6
  36.1 0.2 convert_reduce_fusion
  36.3 0.9 scatter_custom_fusion
  37.2 0.0 copy-done
  37.2 0.0 copy-start.1
  37.2 3.0 %gather_fusion.1 = bf16[128,128,128]{2,1,0:T(8,128)(2,1)} fusion(bf16[96,128,128]{2,1,0:T(8,128)(2,1)S(1)} %copy-done, s32[1024]{0:T(1024)S(1)} %pad_clamp_fusion.1), kind=kCustom, calls=%fused_computation.1 | custom fusion | bytes 8389120 | tf_op jit(solution)/shard_map/jit(_take)/gather | solution.py:29
  40.2 0.0 copy-done.1
  40.2 12.8 %all-gather.1 = bf16[8,1,128,128]{3,2,1,0:T(8,128)(2,1)S(1)} all-gather(bf16[1,1,128,128]{3,2,1,0:T(8,128)(2,1)S(1)} %copy-done.1), channel_id=3, replica_groups=mesh['y'=8,'z'=8,'mpo'=8] {'mpo'}, dimensions={0}, use_global_device_ids=true | all-gather | bytes 294912 | tf_op jit(solution)/shard_map/all_gather | solution.py:20
  53.1 20.4 %all-gather.4.cloned.1.call-done = bf16[512,16,128]{2,1,0:T(8,128)(2,1)} async-done(((bf16[64,16,128]{2,1,0:T(8,128)(2,1)}), bf16[512,16,128]{2,1,0:T(8,128)(2,1)}) %all-gather.4.cloned.1.call-update) | async-done | bytes 2097168 | tf_op jit(solution)/shard_map/all_gather | solution.py:18
  73.5 4.1 %convolution_convert_fusion = bf16[64,2,128,128]{2,3,1,0:T(8,128)(2,1)S(1)} fusion(bf16[64,2,128,128]{3,2,1,0:T(8,128)(2,1)} %bitcast.47, bf16[64,128,128,1]{2,1,3,0:T(8,128)(2,1)} %bitcast.49), kind=kOutput, calls=%fused_computation.4 | convolution fusion | flops 538968064 | bytes 10485760 | tf_op jit(solution)/shard_map/prk,psjk->psrj/dot_general | solution.py:30
  77.6 2.0 %fusion = bf16[64,2,16,128]{3,2,1,0:T(8,128)(2,1)} fusion(bf16[64,2,8,16,128]{4,3,2,1,0:T(8,128)(2,1)S(1)} %bitcast.48, bf16[8,1,128,128]{3,2,1,0:T(8,128)(2,1)S(1)} %all-gather.1), kind=kOutput, calls=%fused_computation.6 | convolution fusion | flops 537133056 | bytes 4980736 | tf_op jit(solution)/shard_map/pswcj,wij->psci/dot_general | solution.py:32
  79.6 2.4 %gather_fusion.2 = bf16[96,16,128]{2,1,0:T(8,128)(2,1)} fusion(bf16[128,16,128]{2,1,0:T(8,128)(2,1)} %bitcast.50, s32[1024]{0:T(1024)S(1)} %pad_clamp_fusion), kind=kCustom, calls=%fused_computation.2 | custom fusion | bytes 786816 | tf_op jit(solution)/shard_map/jit(_take)/gather | solution.py:33
  (6 shorter events, 0.0 us)
Async XLA Ops:
  6.5 30.6 %copy-start = (bf16[96,128,128]{2,1,0:T(8,128)(2,1)S(1)}, bf16[96,128,128]{2,1,0:T(8,128)(2,1)}, u32[]{:S(2)}) copy-start(bf16[96,128,128]{2,1,0:T(8,128)(2,1)} %param.5) | copy-start | bytes 9437188
  6.5 66.9 %all-gather.4.cloned.1.call-start = ((), (), s32[]{:S(2)}) async-start(), calls=%async_computation.1 | async-start | bytes 2359296 | tf_op jit(solution)/shard_map/all_gather | solution.py:18
  37.2 3.0 %copy-start.1 = (bf16[1,1,128,128]{3,2,1,0:T(8,128)(2,1)S(1)}, bf16[1,1,128,128]{3,2,1,0:T(8,128)(2,1)}, u32[]{:S(2)}) copy-start(bf16[1,1,128,128]{3,2,1,0:T(8,128)(2,1)} %param.6) | copy-start | bytes 98308
Sparse Core Ops, SparseCore 0:
  33.3 40.1 all-gather.3

commit v6 on v5

--- a/solution.py
+++ b/solution.py
@@ -30,8 +30,10 @@
     inner = jnp.einsum("prk,psjk->psrj", table, slotted, preferred_element_type=jnp.float32)
     inner = inner.astype(jnp.bfloat16).reshape(rows, cap, terms, width, size)
     out = jnp.einsum("pswcj,wij->psci", inner, lefts, preferred_element_type=jnp.float32)
-    out = jnp.take(out.astype(jnp.bfloat16).reshape(rows * cap, width, size), slot, axis=0, mode="clip")
-    return jnp.swapaxes(out, 1, 2)
+    out = out.astype(jnp.bfloat16).reshape(rows * cap, width * size)
+    pick = (slot[:, None] == jnp.arange(rows * cap)[None, :]).astype(jnp.bfloat16)
+    out = jnp.dot(pick, out, preferred_element_type=jnp.float32).astype(jnp.bfloat16)
+    return jnp.swapaxes(out.reshape(blocks, width, size), 1, 2)
 
 
 def solution(mesh):

time: 89.1 us -> 87 us (0.976)
  local copies, waits for them, and re-layouts: 8.87 us -> 7.24 us
    gather x1 -> x0, local copies, waits for them, and re-layouts: 2.44 us -> none  [local(): jnp.take(out.astype(jnp.bfloat16).reshape(rows * cap, width, size), slot,...]
where the time goes in v6:
time: 87 us; the launch traced here: 86.9 us
  blocking collectives  38.5 us (44%)
  waiting for transfers between devices  20.4 us (23%)
  between operations  13.5 us (16%)
  local copies, waits for them, and re-layouts  7.24 us (8%)
  matrix products  5.7 us (7%)
  other arithmetic  1.53 us (2%)
    all_to_all x1, blocking collectives, local(): row = lax.all_to_all(spread, ('z', 'mpo'), 0, 0, tiled=True)  25.6 us
    all_gather x1, waiting for transfers between devices, local(): table = lax.all_gather(row, 'y', axis=0, tiled=False)  20.4 us
    all_gather x1, blocking collectives, local(): lefts = lax.all_gather(left_env[0, 0], 'mpo', axis=0, tiled=False)  12.8 us
    dot_general x1, matrix products, local(): jnp.einsum('prk,psjk->psrj', table, slotted, preferred_element_type=jnp.f...  4.12 us
    gather x1, local copies, waits for them, and re-layouts, local(): jnp.take(wave, owner, axis=0, mode='clip').reshape(rows, cap, size, size)  3.02 us
  transfers between devices with their start and end apart: 1, of which 1 were waited for; matrix products, arithmetic and copies ran while one was open for 8% of the time, Pallas kernels for 0%

profile of v6, /device:TPU:6, one launch (start us, length us, event | category | flops | bytes accessed | tf_op | source)
XLA Modules:
  0.0 86.9 jit_solution(15202228125537252326)
XLA Ops:
  6.5 0.0 copy-start
  6.5 0.0 all-gather.4.cloned.1.call-start
  6.5 0.9 %broadcast_in_dim.34 = bf16[8,8,16,128]{3,2,1,0:T(8,128)(2,1)S(1)} broadcast(bf16[8,16,128]{2,1,0:T(8,128)(2,1)} %bitcast.60), dimensions={1,2,3} | broadcast | bytes 294912 | tf_op jit(solution)/shard_map/broadcast_in_dim | solution.py:16
  7.5 25.6 %all_to_all.5 = bf16[64,16,128]{2,1,0:T(8,128)(2,1)} all-to-all(bf16[64,16,128]{2,1,0:T(8,128)(2,1)S(1)} %bitcast.59), channel_id=1, replica_groups=mesh['y'=8,'z'=8,'mpo'=8] {'z','mpo'}, dimensions={0} | all-to-all | bytes 524288 | tf_op jit(solution)/shard_map/all_to_all | solution.py:17
  33.1 0.0 all-gather.4.cloned.1.call-update
  33.2 0.7 fusion.11
  33.8 1.6 %gather_fusion = s32[96]{0:T(128)S(1)} fusion(s32[64]{0:T(128)} %param.9, s32[1024]{0:T(1024)S(1)} %pad_clamp_fusion.1), kind=kCustom, calls=%fused_computation | custom fusion | bytes 1152 | tf_op jit(solution)/shard_map/jit(_take)/gather | solution.py:21
  35.4 0.7 fusion.10
  36.1 0.2 convert_reduce_fusion
  36.3 0.9 %scatter_custom_fusion = s32[128]{0:T(128)S(1)} fusion(s32[96]{0:T(128)S(1)} %get-tuple-element.5, s32[96]{0:T(128)S(1)} %iota.13, s32[]{:T(128)} %constant.22.clone.1), kind=kCustom, calls=%fused_computation.25 | custom fusion | bytes 516 | tf_op jit(solution)/shard_map/scatter | solution.py:28
  37.2 0.0 copy-done
  37.2 0.0 copy-start.1
  37.2 3.0 %gather_fusion.1 = bf16[128,128,128]{2,1,0:T(8,128)(2,1)} fusion(bf16[96,128,128]{2,1,0:T(8,128)(2,1)S(1)} %copy-done, s32[1024]{0:T(1024)S(1)} %pad_clamp_fusion), kind=kCustom, calls=%fused_computation.1 | custom fusion | bytes 8389120 | tf_op jit(solution)/shard_map/jit(_take)/gather | solution.py:29
  40.2 0.0 copy-done.1
  40.2 12.8 %all-gather.1 = bf16[8,1,128,128]{3,2,1,0:T(8,128)(2,1)S(1)} all-gather(bf16[1,1,128,128]{3,2,1,0:T(8,128)(2,1)S(1)} %copy-done.1), channel_id=3, replica_groups=mesh['y'=8,'z'=8,'mpo'=8] {'mpo'}, dimensions={0}, use_global_device_ids=true | all-gather | bytes 294912 | tf_op jit(solution)/shard_map/all_gather | solution.py:20
  53.0 20.4 %all-gather.4.cloned.1.call-done = bf16[512,16,128]{2,1,0:T(8,128)(2,1)} async-done(((bf16[64,16,128]{2,1,0:T(8,128)(2,1)}), bf16[512,16,128]{2,1,0:T(8,128)(2,1)}) %all-gather.4.cloned.1.call-update) | async-done | bytes 2097168 | tf_op jit(solution)/shard_map/all_gather | solution.py:18
  73.5 4.1 %convolution_convert_fusion = bf16[64,2,128,128]{2,3,1,0:T(8,128)(2,1)S(1)} fusion(bf16[64,2,128,128]{3,2,1,0:T(8,128)(2,1)} %bitcast.55, bf16[64,128,128,1]{2,1,3,0:T(8,128)(2,1)} %bitcast.57), kind=kOutput, calls=%fused_computation.3 | convolution fusion | flops 538968064 | bytes 10485760 | tf_op jit(solution)/shard_map/prk,psjk->psrj/dot_general | solution.py:30
  77.6 1.3 %fusion = bf16[64,2,16,128]{3,2,1,0:T(8,128)(2,1)S(1)} fusion(bf16[64,2,8,16,128]{4,3,2,1,0:T(8,128)(2,1)S(1)} %bitcast.56, bf16[8,1,128,128]{3,2,1,0:T(8,128)(2,1)S(1)} %all-gather.1), kind=kOutput, calls=%fused_computation.6 | convolution fusion | flops 537133056 | bytes 4980736 | tf_op jit(solution)/shard_map/pswcj,wij->psci/dot_general | solution.py:32
  78.9 0.3 fusion.1
  79.2 0.8 copy.12
  (5 shorter events, 0.0 us)
Async XLA Ops:
  6.5 30.6 %copy-start = (bf16[96,128,128]{2,1,0:T(8,128)(2,1)S(1)}, bf16[96,128,128]{2,1,0:T(8,128)(2,1)}, u32[]{:S(2)}) copy-start(bf16[96,128,128]{2,1,0:T(8,128)(2,1)} %param.5) | copy-start | bytes 9437188
  6.5 66.9 %all-gather.4.cloned.1.call-start = ((), (), s32[]{:S(2)}) async-start(), calls=%async_computation.1 | async-start | bytes 2359296 | tf_op jit(solution)/shard_map/all_gather | solution.py:18
  37.2 3.0 %copy-start.1 = (bf16[1,1,128,128]{3,2,1,0:T(8,128)(2,1)S(1)}, bf16[1,1,128,128]{3,2,1,0:T(8,128)(2,1)}, u32[]{:S(2)}) copy-start(bf16[1,1,128,128]{3,2,1,0:T(8,128)(2,1)} %param.6) | copy-start | bytes 98308
Sparse Core Ops, SparseCore 0:
  33.3 40.1 all-gather.3

commit v7 on v6

--- a/solution.py
+++ b/solution.py
@@ -13,12 +13,14 @@
     size = wave.shape[1]
     width = size // terms
     own = right_env[0, 0].reshape(1, terms, width, size)
-    spread = jnp.broadcast_to(own, (inner_size, terms, width, size)).reshape(inner_size * terms, width, size)
-    row = lax.all_to_all(spread, ("z", "mpo"), 0, 0, tiled=True)
-    table = lax.all_gather(row, "y", axis=0, tiled=False)
+    outer_size = lax.axis_size("y")
+    spread = jnp.broadcast_to(own, (outer_size, terms, width, size)).reshape(outer_size * terms, width, size)
+    row = lax.all_to_all(spread, ("y", "mpo"), 0, 0, tiled=True)
+    table = lax.all_gather(row, "z", axis=0, tiled=False)
     table = table.reshape(-1, terms * width, size)
     lefts = lax.all_gather(left_env[0, 0], "mpo", axis=0, tiled=False)
     places = jnp.take(right_home, right_sector[:, 0], axis=0)
+    places = (places % inner_size) * outer_size + places // inner_size
     blocks = wave.shape[0]
     rows = table.shape[0]
     cap = 2

time: 87 us -> 87.6 us (level)
  blocking collectives: 38.5 us -> 35.2 us
  waiting for transfers between devices: 20.4 us -> 23.5 us
    all_to_all x1, blocking collectives: 25.6 us -> 22.4 us  [local(): row = lax.all_to_all(spread, ('y', 'mpo'), 0, 0, tiled=True)]
    all_gather x1, waiting for transfers between devices: 20.4 us -> 23.5 us  [local(): table = lax.all_gather(row, 'z', axis=0, tiled=False)]
    add x0 -> x2, other arithmetic: none -> 1.35 us  [local(): places = places % inner_size * outer_size + places // inner_size]
  transfers between devices with their start and end apart: 1 -> 1, of which waited for: 1 -> 1; matrix products, arithmetic and copies ran while one was open for 8% -> 9% of each run, Pallas kernels for 0% -> 0%
where the time goes in v7:
time: 87.6 us; the launch traced here: 87.4 us
  blocking collectives  35.2 us (40%)
  waiting for transfers between devices  23.5 us (27%)
  between operations  13.5 us (15%)
  local copies, waits for them, and re-layouts  7.24 us (8%)
  matrix products  5.71 us (7%)
  other arithmetic  2.2 us (3%)
    all_gather x1, waiting for transfers between devices, local(): table = lax.all_gather(row, 'z', axis=0, tiled=False)  23.5 us
    all_to_all x1, blocking collectives, local(): row = lax.all_to_all(spread, ('y', 'mpo'), 0, 0, tiled=True)  22.4 us
    all_gather x1, blocking collectives, local(): lefts = lax.all_gather(left_env[0, 0], 'mpo', axis=0, tiled=False)  12.8 us
    dot_general x1, matrix products, local(): jnp.einsum('prk,psjk->psrj', table, slotted, preferred_element_type=jnp.f...  4.12 us
    gather x1, local copies, waits for them, and re-layouts, local(): jnp.take(wave, owner, axis=0, mode='clip').reshape(rows, cap, size, size)  3.02 us
  transfers between devices with their start and end apart: 1, of which 1 were waited for; matrix products, arithmetic and copies ran while one was open for 9% of the time, Pallas kernels for 0%

profile of v7, /device:TPU:6, one launch (start us, length us, event | category | flops | bytes accessed | tf_op | source)
XLA Modules:
  0.0 87.4 jit_solution(3275669523542212291)
XLA Ops:
  6.5 0.0 copy-start
  6.5 0.0 all-gather.4.cloned.1.call-start
  6.5 0.9 %broadcast_in_dim.34 = bf16[8,8,16,128]{3,2,1,0:T(8,128)(2,1)S(1)} broadcast(bf16[8,16,128]{2,1,0:T(8,128)(2,1)} %bitcast.62), dimensions={1,2,3} | broadcast | bytes 294912 | tf_op jit(solution)/shard_map/broadcast_in_dim | solution.py:17
  7.5 22.4 %all_to_all.5 = bf16[64,16,128]{2,1,0:T(8,128)(2,1)} all-to-all(bf16[64,16,128]{2,1,0:T(8,128)(2,1)S(1)} %bitcast.61), channel_id=1, replica_groups=mesh['y'=8,'z'=8,'mpo'=8] {'y','mpo'}, dimensions={0} | all-to-all | bytes 524288 | tf_op jit(solution)/shard_map/all_to_all | solution.py:18
  29.9 0.0 all-gather.4.cloned.1.call-update
  29.9 0.7 fusion.14
  30.6 1.6 %gather_fusion = s32[96]{0:T(128)S(1)} fusion(s32[64]{0:T(128)} %param.9, s32[1024]{0:T(1024)S(1)} %pad_clamp_fusion.1), kind=kCustom, calls=%fused_computation | custom fusion | bytes 1152 | tf_op jit(solution)/shard_map/jit(_take)/gather | solution.py:22
  32.2 0.7 fusion.8
  32.9 0.7 fusion.10
  33.5 0.2 convert_reduce_fusion
  33.7 0.9 %scatter_custom_fusion = s32[128]{0:T(128)S(1)} fusion(s32[96]{0:T(128)S(1)} %get-tuple-element.6, s32[96]{0:T(128)S(1)} %iota.13, s32[]{:T(128)} %constant.52.clone.1), kind=kCustom, calls=%fused_computation.39 | custom fusion | bytes 516 | tf_op jit(solution)/shard_map/scatter | solution.py:30
  34.6 0.0 copy-done
  34.6 0.0 copy-start.1
  34.7 3.0 %gather_fusion.1 = bf16[128,128,128]{2,1,0:T(8,128)(2,1)} fusion(bf16[96,128,128]{2,1,0:T(8,128)(2,1)S(1)} %copy-done, s32[1024]{0:T(1024)S(1)} %pad_clamp_fusion), kind=kCustom, calls=%fused_computation.1 | custom fusion | bytes 8389120 | tf_op jit(solution)/shard_map/jit(_take)/gather | solution.py:31
  37.7 0.0 copy-done.1
  37.7 12.8 %all-gather.1 = bf16[8,1,128,128]{3,2,1,0:T(8,128)(2,1)S(1)} all-gather(bf16[1,1,128,128]{3,2,1,0:T(8,128)(2,1)S(1)} %copy-done.1), channel_id=3, replica_groups=mesh['y'=8,'z'=8,'mpo'=8] {'mpo'}, dimensions={0}, use_global_device_ids=true | all-gather | bytes 294912 | tf_op jit(solution)/shard_map/all_gather | solution.py:21
  50.5 23.5 %all-gather.4.cloned.1.call-done = bf16[512,16,128]{2,1,0:T(8,128)(2,1)} async-done(((bf16[64,16,128]{2,1,0:T(8,128)(2,1)}), bf16[512,16,128]{2,1,0:T(8,128)(2,1)}) %all-gather.4.cloned.1.call-update) | async-done | bytes 2097168 | tf_op jit(solution)/shard_map/all_gather | solution.py:19
  74.0 4.1 %convolution_convert_fusion = bf16[64,2,128,128]{2,3,1,0:T(8,128)(2,1)S(1)} fusion(bf16[64,2,128,128]{3,2,1,0:T(8,128)(2,1)} %bitcast.57, bf16[64,128,128,1]{2,1,3,0:T(8,128)(2,1)} %bitcast.59), kind=kOutput, calls=%fused_computation.3 | convolution fusion | flops 538968064 | bytes 10485760 | tf_op jit(solution)/shard_map/prk,psjk->psrj/dot_general | solution.py:32
  78.1 1.3 %fusion = bf16[64,2,16,128]{3,2,1,0:T(8,128)(2,1)S(1)} fusion(bf16[64,2,8,16,128]{4,3,2,1,0:T(8,128)(2,1)S(1)} %bitcast.58, bf16[8,1,128,128]{3,2,1,0:T(8,128)(2,1)S(1)} %all-gather.1), kind=kOutput, calls=%fused_computation.6 | convolution fusion | flops 537133056 | bytes 4980736 | tf_op jit(solution)/shard_map/pswcj,wij->psci/dot_general | solution.py:34
  79.4 0.3 fusion.1
  79.7 0.8 copy.12
  (4 shorter events, 0.0 us)
Async XLA Ops:
  6.5 28.1 %copy-start = (bf16[96,128,128]{2,1,0:T(8,128)(2,1)S(1)}, bf16[96,128,128]{2,1,0:T(8,128)(2,1)}, u32[]{:S(2)}) copy-start(bf16[96,128,128]{2,1,0:T(8,128)(2,1)} %param.5) | copy-start | bytes 9437188
  6.5 67.5 %all-gather.4.cloned.1.call-start = ((), (), s32[]{:S(2)}) async-start(), calls=%async_computation.1 | async-start | bytes 2359296 | tf_op jit(solution)/shard_map/all_gather | solution.py:19
  34.6 3.0 %copy-start.1 = (bf16[1,1,128,128]{3,2,1,0:T(8,128)(2,1)S(1)}, bf16[1,1,128,128]{3,2,1,0:T(8,128)(2,1)}, u32[]{:S(2)}) copy-start(bf16[1,1,128,128]{3,2,1,0:T(8,128)(2,1)} %param.6) | copy-start | bytes 98308
Sparse Core Ops, SparseCore 0:
  30.1 43.8 all-gather.3

commit v8 on v6

--- a/solution.py
+++ b/solution.py
@@ -8,16 +8,22 @@
 
 
 def local(wave, left_env, right_env, right_sector, right_home):
-    terms = lax.axis_size("mpo")
+    terms = lax.axis_size(("x", "c"))
     inner_size = lax.axis_size("z")
     size = wave.shape[1]
     width = size // terms
-    own = right_env[0, 0].reshape(1, terms, width, size)
-    spread = jnp.broadcast_to(own, (inner_size, terms, width, size)).reshape(inner_size * terms, width, size)
-    row = lax.all_to_all(spread, ("z", "mpo"), 0, 0, tiled=True)
+    cores = lax.axis_size("c")
+    core = lax.axis_index("c")
+    own = right_env[0, 0].reshape(terms // cores, cores, width, size)
+    keep = jnp.where(core == 0, own[:, 0], own[:, 1])
+    give = jnp.where(core == 0, own[:, 1], own[:, 0])
+    got = lax.ppermute(give, "c", [(0, 1), (1, 0)])
+    pair = jnp.where(core == 0, jnp.stack([keep, got], 1), jnp.stack([got, keep], 1))
+    spread = jnp.broadcast_to(pair[None], (inner_size,) + pair.shape).reshape(-1, cores, width, size)
+    row = lax.all_to_all(spread, ("z", "x"), 0, 0, tiled=True)
     table = lax.all_gather(row, "y", axis=0, tiled=False)
     table = table.reshape(-1, terms * width, size)
-    lefts = lax.all_gather(left_env[0, 0], "mpo", axis=0, tiled=False)
+    lefts = lax.all_gather(left_env[0, 0], ("x", "c"), axis=0, tiled=False)
     places = jnp.take(right_home, right_sector[:, 0], axis=0)
     blocks = wave.shape[0]
     rows = table.shape[0]
@@ -39,14 +45,15 @@
 def solution(mesh):
     blocks, terms = mesh.devices.shape
     inner_size = math.isqrt(blocks)
-    grid = Mesh(mesh.devices.reshape(blocks // inner_size, inner_size, terms), ("y", "z", "mpo"))
+    grid = Mesh(mesh.devices.reshape(blocks // inner_size, inner_size, terms // 2, 2), ("y", "z", "x", "c"))
     blk = ("y", "z")
+    mpo = ("x", "c")
     in_specs = (
         P(blk, None, None),
-        P("mpo", blk, None, None),
-        P("mpo", blk, None, None),
+        P(mpo, blk, None, None),
+        P(mpo, blk, None, None),
         P(blk, None),
         P(),
     )
-    out_specs = P(blk, None, "mpo")
+    out_specs = P(blk, None, mpo)
     return jax.shard_map(local, mesh=grid, in_specs=in_specs, out_specs=out_specs, check_vma=False)

time: 87 us -> 89.6 us (1.030)
  starting transfers between devices: 0.01 us -> 2.04 us
  other arithmetic: 1.53 us -> 3.17 us
    ppermute x0 -> x1, starting transfers between devices: none -> 2.04 us  [local(): got = lax.ppermute(give, 'c', [(0, 1), (1, 0)])]
    select_n x0 -> x3, other arithmetic: none -> 1.64 us  [the longest x1 0.89 us: local(): give = jnp.where(core == 0, own[:, 1], own[:, 0])]
    broadcast_in_dim x1, local copies, waits for them, and re-layouts: 0.94 us -> 0.04 us  [local(): jnp.broadcast_to(pair[None], (inner_size,) + pair.shape)]
  transfers between devices with their start and end apart: 1 -> 2, of which waited for: 1 -> 2; matrix products, arithmetic and copies ran while one was open for 8% -> 9% of each run, Pallas kernels for 0% -> 0%
where the time goes in v8:
time: 89.6 us; the launch traced here: 89.3 us
  blocking collectives  37.7 us (42%)
  waiting for transfers between devices  20.9 us (23%)
  between operations  13.5 us (15%)
  local copies, waits for them, and re-layouts  6.35 us (7%)
  matrix products  5.71 us (6%)
  other arithmetic  3.17 us (4%)
  starting transfers between devices  2.04 us (2%)
    all_to_all x1, blocking collectives, local(): row = lax.all_to_all(spread, ('z', 'x'), 0, 0, tiled=True)  24.9 us
    all_gather x1, waiting for transfers between devices, local(): table = lax.all_gather(row, 'y', axis=0, tiled=False)  20.5 us
    all_gather x1, blocking collectives, local(): lefts = lax.all_gather(left_env[0, 0], ('x', 'c'), axis=0, tiled=False)  12.8 us
    dot_general x1, matrix products, local(): jnp.einsum('prk,psjk->psrj', table, slotted, preferred_element_type=jnp.f...  4.12 us
    gather x1, local copies, waits for them, and re-layouts, local(): jnp.take(wave, owner, axis=0, mode='clip').reshape(rows, cap, size, size)  3.03 us
    ppermute x1, starting transfers between devices, local(): got = lax.ppermute(give, 'c', [(0, 1), (1, 0)])  2.04 us
  transfers between devices with their start and end apart: 2, of which 2 were waited for; matrix products, arithmetic and copies ran while one was open for 9% of the time, Pallas kernels for 0%

profile of v8, /device:TPU:6, one launch (start us, length us, event | category | flops | bytes accessed | tf_op | source)
XLA Modules:
  0.0 89.3 jit_solution(11269587284188683627)
XLA Ops:
  6.5 0.0 copy-start
  6.5 0.0 all-gather.4.cloned.1.call-start
  6.5 0.9 fusion.7
  7.4 2.0 %collective-permute-start = (bf16[4,16,128]{2,1,0:T(8,128)(2,1)S(1)}, bf16[4,16,128]{2,1,0:T(8,128)(2,1)S(1)}, u32[]{:S(2)}, u32[]{:S(2)}) collective-permute-start(bf16[4,16,128]{2,1,0:T(8,128)(2,1)S(1)} %fusion.7), channel_id=1, source_target_pairs={{0,1},{1,0},{2,3},{3,2},{4,5},{5,4},{6,7},{7,6},{8,9},{9,8},{10,11... | collective-permute-start | bytes 49160 | tf_op jit(solution)/shard_map/ppermute | solution.py:20
  9.5 0.7 bitcast_select_fusion.1
  10.2 0.4 collective-permute-done
  10.7 24.9 %all_to_all.5 = bf16[32,2,16,128]{3,2,1,0:T(8,128)(2,1)} all-to-all(bf16[32,2,16,128]{3,2,1,0:T(8,128)(2,1)S(1)} %bitcast.72), channel_id=1, replica_groups=mesh['y'=8,'z'=8,'x'=4,'c'=2] {'z','x'}, dimensions={0} | all-to-all | bytes 524288 | tf_op jit(solution)/shard_map/all_to_all | solution.py:23
  35.6 0.0 all-gather.4.cloned.1.call-update
  35.6 0.7 fusion.12
  36.3 1.6 %gather_fusion = s32[96]{0:T(128)S(1)} fusion(s32[64]{0:T(128)} %param.9, s32[1024]{0:T(1024)S(1)} %pad_clamp_fusion.1), kind=kCustom, calls=%fused_computation | custom fusion | bytes 1152 | tf_op jit(solution)/shard_map/jit(_take)/gather | solution.py:27
  37.8 0.7 fusion.11
  38.5 0.2 convert_reduce_fusion
  38.7 0.9 scatter_custom_fusion
  39.6 0.0 copy-done
  39.6 0.0 copy-start.1
  39.6 3.0 %gather_fusion.1 = bf16[128,128,128]{2,1,0:T(8,128)(2,1)} fusion(bf16[96,128,128]{2,1,0:T(8,128)(2,1)S(1)} %copy-done, s32[1024]{0:T(1024)S(1)} %pad_clamp_fusion), kind=kCustom, calls=%fused_computation.1 | custom fusion | bytes 8389120 | tf_op jit(solution)/shard_map/jit(_take)/gather | solution.py:35
  42.7 0.0 copy-done.1
  42.7 12.8 %all-gather.1 = bf16[8,1,128,128]{3,2,1,0:T(8,128)(2,1)S(1)} all-gather(bf16[1,1,128,128]{3,2,1,0:T(8,128)(2,1)S(1)} %copy-done.1), channel_id=3, replica_groups=mesh['y'=8,'z'=8,'x'=4,'c'=2] {'x','c'}, dimensions={0}, use_global_device_ids=true | all-gather | bytes 294912 | tf_op jit(solution)/shard_map/all_gather | solution.py:26
  55.5 20.5 %all-gather.4.cloned.1.call-done = bf16[256,2,16,128]{3,2,1,0:T(8,128)(2,1)} async-done(((bf16[32,2,16,128]{3,2,1,0:T(8,128)(2,1)}), bf16[256,2,16,128]{3,2,1,0:T(8,128)(2,1)}) %all-gather.4.cloned.1.call-update) | async-done | bytes 2097168 | tf_op jit(solution)/shard_map/all_gather | solution.py:24
  75.9 4.1 %convolution_convert_fusion = bf16[64,2,128,128]{2,3,1,0:T(8,128)(2,1)S(1)} fusion(bf16[64,2,128,128]{3,2,1,0:T(8,128)(2,1)} %bitcast.68, bf16[64,128,128,1]{2,1,3,0:T(8,128)(2,1)} %bitcast.70), kind=kOutput, calls=%fused_computation.3 | convolution fusion | flops 538968064 | bytes 10485760 | tf_op jit(solution)/shard_map/prk,psjk->psrj/dot_general | solution.py:36
  80.1 1.3 %fusion = bf16[64,2,16,128]{3,2,1,0:T(8,128)(2,1)S(1)} fusion(bf16[64,2,8,16,128]{4,3,2,1,0:T(8,128)(2,1)S(1)} %bitcast.69, bf16[8,1,128,128]{3,2,1,0:T(8,128)(2,1)S(1)} %all-gather.1), kind=kOutput, calls=%fused_computation.6 | convolution fusion | flops 537133056 | bytes 4980736 | tf_op jit(solution)/shard_map/pswcj,wij->psci/dot_general | solution.py:38
  81.3 0.3 fusion.1
  81.7 0.8 copy.33
  (8 shorter events, 0.1 us)
Async XLA Ops:
  6.5 33.1 %copy-start = (bf16[96,128,128]{2,1,0:T(8,128)(2,1)S(1)}, bf16[96,128,128]{2,1,0:T(8,128)(2,1)}, u32[]{:S(2)}) copy-start(bf16[96,128,128]{2,1,0:T(8,128)(2,1)} %param.5) | copy-start | bytes 9437188
  6.5 69.4 %all-gather.4.cloned.1.call-start = ((), (), s32[]{:S(2)}) async-start(), calls=%async_computation.1 | async-start | bytes 2359296 | tf_op jit(solution)/shard_map/all_gather | solution.py:24
  7.4 3.2 %collective-permute-start = (bf16[4,16,128]{2,1,0:T(8,128)(2,1)S(1)}, bf16[4,16,128]{2,1,0:T(8,128)(2,1)S(1)}, u32[]{:S(2)}, u32[]{:S(2)}) collective-permute-start(bf16[4,16,128]{2,1,0:T(8,128)(2,1)S(1)} %fusion.7), channel_id=1, source_target_pairs={{0,1},{1,0},{2,3},{3,2},{4,5},{5,4},{6,7},{7,6},{8,9},{9,8},{10,11... | collective-permute-start | bytes 49160 | tf_op jit(solution)/shard_map/ppermute | solution.py:20
  39.6 3.0 %copy-start.1 = (bf16[1,1,128,128]{3,2,1,0:T(8,128)(2,1)S(1)}, bf16[1,1,128,128]{3,2,1,0:T(8,128)(2,1)}, u32[]{:S(2)}) copy-start(bf16[1,1,128,128]{3,2,1,0:T(8,128)(2,1)} %param.6) | copy-start | bytes 98308
Sparse Core Ops, SparseCore 0:
  35.7 40.1 all-gather.3

commit v9 on v6

--- a/solution.py
+++ b/solution.py
@@ -12,9 +12,10 @@
     inner_size = lax.axis_size("z")
     size = wave.shape[1]
     width = size // terms
-    own = right_env[0, 0].reshape(1, terms, width, size)
-    spread = jnp.broadcast_to(own, (inner_size, terms, width, size)).reshape(inner_size * terms, width, size)
-    row = lax.all_to_all(spread, ("z", "mpo"), 0, 0, tiled=True)
+    own = right_env[0, 0].reshape(terms, 1, width, size)
+    spread = jnp.broadcast_to(own, (terms, inner_size, width, size)).reshape(terms * inner_size, width, size)
+    row = lax.all_to_all(spread, ("mpo", "z"), 0, 0, tiled=True)
+    row = jnp.swapaxes(row.reshape(terms, inner_size, width, size), 0, 1).reshape(-1, width, size)
     table = lax.all_gather(row, "y", axis=0, tiled=False)
     table = table.reshape(-1, terms * width, size)
     lefts = lax.all_gather(left_env[0, 0], "mpo", axis=0, tiled=False)

time: 87 us -> 87.8 us (level)
  no operation moved by 1% of the time
where the time goes in v9:
time: 87.8 us; the launch traced here: 87.7 us
  blocking collectives  38 us (43%)
  waiting for transfers between devices  21 us (24%)
  between operations  13.5 us (15%)
  local copies, waits for them, and re-layouts  7.96 us (9%)
  matrix products  5.7 us (6%)
  other arithmetic  1.53 us (2%)
    all_to_all x1, blocking collectives, local(): row = lax.all_to_all(spread, ('mpo', 'z'), 0, 0, tiled=True)  25.2 us
    all_gather x1, waiting for transfers between devices, local(): table = lax.all_gather(row, 'y', axis=0, tiled=False)  21 us
    all_gather x1, blocking collectives, local(): lefts = lax.all_gather(left_env[0, 0], 'mpo', axis=0, tiled=False)  12.8 us
    dot_general x1, matrix products, local(): jnp.einsum('prk,psjk->psrj', table, slotted, preferred_element_type=jnp.f...  4.12 us
    gather x1, local copies, waits for them, and re-layouts, local(): jnp.take(wave, owner, axis=0, mode='clip').reshape(rows, cap, size, size)  3.02 us
  transfers between devices with their start and end apart: 1, of which 1 were waited for; matrix products, arithmetic and copies ran while one was open for 8% of the time, Pallas kernels for 0%

profile of v9, /device:TPU:6, one launch (start us, length us, event | category | flops | bytes accessed | tf_op | source)
XLA Modules:
  0.0 87.7 jit_solution(937695591468631218)
XLA Ops:
  6.5 0.0 copy-start
  6.5 0.0 all-gather.3.cloned.1.call-start
  6.5 0.9 %broadcast_in_dim.34 = bf16[8,8,16,128]{3,2,1,0:T(8,128)(2,1)S(1)} broadcast(bf16[8,16,128]{2,1,0:T(8,128)(2,1)} %bitcast.66), dimensions={0,2,3} | broadcast | bytes 294912 | tf_op jit(solution)/shard_map/broadcast_in_dim | solution.py:16
  7.5 25.2 %all_to_all.5 = bf16[64,16,128]{2,1,0:T(8,128)(2,1)S(1)} all-to-all(bf16[64,16,128]{2,1,0:T(8,128)(2,1)S(1)} %bitcast.65), channel_id=1, replica_groups=mesh['y'=8,'z'=8,'mpo'=8] {'mpo','z'}, dimensions={0} | all-to-all | bytes 524288 | tf_op jit(solution)/shard_map/all_to_all | solution.py:17
  32.7 0.7 copy.11
  33.4 0.0 all-gather.3.cloned.1.call-update
  33.4 0.7 fusion.11
  34.1 1.6 %gather_fusion = s32[96]{0:T(128)S(1)} fusion(s32[64]{0:T(128)} %param.9, s32[1024]{0:T(1024)S(1)} %pad_clamp_fusion.1), kind=kCustom, calls=%fused_computation | custom fusion | bytes 1152 | tf_op jit(solution)/shard_map/jit(_take)/gather | solution.py:22
  35.7 0.7 fusion.10
  36.4 0.2 convert_reduce_fusion
  36.6 0.9 scatter_custom_fusion
  37.5 0.0 copy-done
  37.5 0.0 copy-start.1
  37.5 3.0 %gather_fusion.1 = bf16[128,128,128]{2,1,0:T(8,128)(2,1)} fusion(bf16[96,128,128]{2,1,0:T(8,128)(2,1)S(1)} %copy-done, s32[1024]{0:T(1024)S(1)} %pad_clamp_fusion), kind=kCustom, calls=%fused_computation.1 | custom fusion | bytes 8389120 | tf_op jit(solution)/shard_map/jit(_take)/gather | solution.py:30
  40.5 0.0 copy-done.1
  40.5 12.8 %all-gather = bf16[8,1,128,128]{3,2,1,0:T(8,128)(2,1)S(1)} all-gather(bf16[1,1,128,128]{3,2,1,0:T(8,128)(2,1)S(1)} %copy-done.1), channel_id=2, replica_groups=mesh['y'=8,'z'=8,'mpo'=8] {'mpo'}, dimensions={0}, use_global_device_ids=true | all-gather | bytes 294912 | tf_op jit(solution)/shard_map/all_gather | solution.py:21
  53.3 21.0 %all-gather.3.cloned.1.call-done = bf16[8,64,16,128]{3,2,1,0:T(8,128)(2,1)} async-done(((bf16[1,64,16,128]{3,2,1,0:T(8,128)(2,1)}), bf16[8,64,16,128]{3,2,1,0:T(8,128)(2,1)}) %all-gather.3.cloned.1.call-update) | async-done | bytes 2097168 | tf_op jit(solution)/shard_map/all_gather | solution.py:19
  74.3 4.1 %convolution_convert_fusion = bf16[64,2,128,128]{2,3,1,0:T(8,128)(2,1)S(1)} fusion(bf16[64,2,128,128]{3,2,1,0:T(8,128)(2,1)} %bitcast.59, bf16[64,128,128,1]{2,1,3,0:T(8,128)(2,1)} %bitcast.61), kind=kOutput, calls=%fused_computation.3 | convolution fusion | flops 538968064 | bytes 10485760 | tf_op jit(solution)/shard_map/prk,psjk->psrj/dot_general | solution.py:31
  78.4 1.3 %fusion = bf16[64,2,16,128]{3,2,1,0:T(8,128)(2,1)S(1)} fusion(bf16[64,2,8,16,128]{4,3,2,1,0:T(8,128)(2,1)S(1)} %bitcast.60, bf16[8,1,128,128]{3,2,1,0:T(8,128)(2,1)S(1)} %all-gather), kind=kOutput, calls=%fused_computation.6 | convolution fusion | flops 537133056 | bytes 4980736 | tf_op jit(solution)/shard_map/pswcj,wij->psci/dot_general | solution.py:33
  79.7 0.3 fusion.1
  80.0 0.8 copy.16
  (5 shorter events, 0.0 us)
Async XLA Ops:
  6.5 30.9 %copy-start = (bf16[96,128,128]{2,1,0:T(8,128)(2,1)S(1)}, bf16[96,128,128]{2,1,0:T(8,128)(2,1)}, u32[]{:S(2)}) copy-start(bf16[96,128,128]{2,1,0:T(8,128)(2,1)} %param.5) | copy-start | bytes 9437188
  6.5 67.8 %all-gather.3.cloned.1.call-start = ((), (), s32[]{:S(2)}) async-start(), calls=%async_computation.1 | async-start | bytes 2359296 | tf_op jit(solution)/shard_map/all_gather | solution.py:19
  37.5 3.0 %copy-start.1 = (bf16[1,1,128,128]{3,2,1,0:T(8,128)(2,1)S(1)}, bf16[1,1,128,128]{3,2,1,0:T(8,128)(2,1)}, u32[]{:S(2)}) copy-start(bf16[1,1,128,128]{3,2,1,0:T(8,128)(2,1)} %param.6) | copy-start | bytes 98308
Sparse Core Ops, SparseCore 0:
  33.5 40.7 all-gather.2
